TPU v7x, 32 devices: a whole 2x2x4 slice. The times are simulated.
32 devices in a mesh: req: 4 (over x, core), head: 8 (over z, y).
Axes of the slice: x: 2, y: 2, z: 4, core: 2. Of those that a mesh axis runs over, the one named last changes fastest.
Arguments:
- stretch_acts: bfloat16 [8, 256, 2048], P(None, ('req', 'head')), may hold values from -6 to 6
- cache_prefill: bfloat16 [8, 8, 256, 32, 128], P('req', None, 'head'), may hold values from -600 to 600
- stretch_lens: int32 [8], replicated, may hold values from 1 to 256, 1280 in all
- prefix_lens: int32 [8], replicated, may hold values from 1 to 256, 1280 in all
- req_order: int32 [8], replicated, may hold values from 0 to 7, each once
- attn_gain: bfloat16 [2048], replicated, may hold values from 0.25 to 1.75
- in_weight: bfloat16 [2048, 32, 192], P(None, 'head'), may hold values from -0.125 to 0.125
- slopes: float32 [32], P('head'), may hold values from 0.00390625 to 0.5
- out_weight: bfloat16 [32, 64, 2048], P('head'), may hold values from -0.125 to 0.125
- mlp_gain: bfloat16 [2048], replicated, may hold values from 0.25 to 1.75
- up_weight: bfloat16 [2048, 8192], P(None, 'head'), may hold values from -0.125 to 0.125
- down_weight: bfloat16 [8192, 2048], P('head'), may hold values from -0.0625 to 0.0625
Outputs:
- layer_out: bfloat16 [8, 256, 2048], P(None, ('req', 'head'))
- cache_decode: bfloat16 [8, 8, 256, 32, 128], P(None, 'req', None, 'head')
Inputs may be any that keep to these rules, and one draw needn't show every extreme that they name: `stretch_lens`: the entries sum to 1280 and the largest is exactly 256. `prefix_lens`: the entries sum to 1280 and the largest is exactly 256. `req_order`: each request appears once.
All inputs are finite; a program needn't handle non-finite values.
Results may differ from a plain program's by a relative error of at most 0.013.
The roundings to bfloat16 on the way count: a program that leaves them out, or rounds other values in their place, can miss the bound.
Values may be sent and summed in bfloat16 or wider, within the bound.
No kernel may reach another device: no remote copies, remote signals or barrier semaphores. Data moves between devices by JAX's collectives and lax.ppermute only.
A program may use at most 128 MiB of HBM per device.

v0:
```python
import math
import jax
import jax.numpy as jnp
from jax import lax
from jax.sharding import PartitionSpec as P

EPSILON = 1e-05


def layer_norm(values, gain):
    average = jnp.mean(values, axis=-1, keepdims=True)
    centred = values - average
    variance = jnp.mean(centred * centred, axis=-1, keepdims=True)
    return centred * lax.rsqrt(variance + EPSILON) * gain.astype(jnp.float32)


def attend(queries, pairs, prefix_len, slopes, head_dim):
    stretch = queries.shape[0]
    prefix = pairs.shape[0] - stretch
    keys_part = pairs[..., :head_dim]
    values_part = pairs[..., head_dim:]
    scores = jnp.einsum("qhd,khd->hqk", queries, keys_part, preferred_element_type=jnp.float32) * (
        1.0 / math.sqrt(head_dim)
    )
    row_index = jnp.arange(stretch, dtype=jnp.int32)
    key_index = jnp.arange(prefix + stretch, dtype=jnp.int32)
    in_prefix = key_index < prefix
    query_pos = prefix_len + row_index
    key_pos = jnp.where(in_prefix, key_index, prefix_len + key_index - prefix)
    allowed = jnp.where(
        in_prefix[None, :],
        key_index[None, :] < prefix_len,
        (key_index - prefix)[None, :] <= row_index[:, None],
    )
    distance = (query_pos[:, None] - key_pos[None, :]).astype(jnp.float32)
    scores = scores - slopes[:, None, None] * distance[None]
    scores = jnp.where(allowed[None], scores, -jnp.inf)
    highest = jnp.max(scores, axis=-1, keepdims=True)
    expo = jnp.exp(scores - highest)
    soft = (expo / jnp.sum(expo, axis=-1, keepdims=True)).astype(jnp.bfloat16)
    context = jnp.einsum("hqk,khd->qhd", soft, values_part, preferred_element_type=jnp.float32)
    return context.astype(jnp.bfloat16).reshape(stretch, -1)


def local(
    stretch_acts,
    cache_prefill,
    stretch_lens,
    prefix_lens,
    req_order,
    attn_gain,
    in_weight,
    slopes,
    out_weight,
    mlp_gain,
    up_weight,
    down_weight,
):
    req_count = lax.axis_size("req")
    head_count = lax.axis_size("head")
    req_index = lax.axis_index("req")
    head_index = lax.axis_index("head")
    requests = stretch_acts.shape[0]
    stretch_rows = stretch_acts.shape[1]
    features = stretch_acts.shape[2]
    group_size = requests // req_count
    span_rows = head_count * stretch_rows
    stretch_max = req_count * span_rows
    prefix_rows = cache_prefill.shape[2]
    heads_here = in_weight.shape[1]
    pair_width = cache_prefill.shape[4]
    head_dim = pair_width // 2
    members = lax.dynamic_slice_in_dim(req_order, req_index * group_size, group_size)
    member_stretch = jnp.take(stretch_lens, members)
    member_prefix = jnp.take(prefix_lens, members)
    ordered_prefix = jnp.take(prefix_lens, req_order)
    positions = head_index * prefix_rows + jnp.arange(prefix_rows, dtype=jnp.int32)
    keep = positions[None, :] < ordered_prefix[:, None]
    local_layers = cache_prefill.shape[0]
    halves = []
    for layer in range(local_layers):
        dealt_cache = jnp.where(
            keep[None, :, :, None, None],
            jnp.take(cache_prefill[layer : layer + 1], req_order, axis=1),
            jnp.zeros((), cache_prefill.dtype),
        )
        halves.append(
            lax.all_to_all(
                lax.all_to_all(dealt_cache, "head", split_axis=3, concat_axis=2, tiled=True),
                "req",
                split_axis=1,
                concat_axis=0,
                tiled=True,
            )
        )
    current = halves[0][0]
    relaid = jnp.stack(halves, axis=1).reshape((req_count * local_layers,) + halves[0].shape[1:])
    dealt_acts = jnp.take(stretch_acts, req_order, axis=0)
    dealt_rows = lax.all_to_all(dealt_acts, "req", split_axis=0, concat_axis=1, tiled=True).reshape(
        group_size, req_count, stretch_rows, features
    )
    gathered = lax.all_gather(dealt_rows, "head", axis=2, tiled=True)
    normed = (
        layer_norm(gathered.astype(jnp.float32), attn_gain)
        .astype(jnp.bfloat16)
        .reshape(group_size * stretch_max, features)
    )
    mixed = jnp.dot(
        normed,
        in_weight.reshape(features, heads_here * 3 * head_dim),
        preferred_element_type=jnp.float32,
    )
    mixed = mixed.reshape(group_size, stretch_max, heads_here, 3 * head_dim).astype(jnp.bfloat16)
    contexts = []
    for member in range(group_size):
        pairs = jnp.concatenate([current[member], mixed[member, :, :, head_dim:]], axis=0)
        contexts.append(
            attend(mixed[member, :, :, :head_dim], pairs, member_prefix[member], slopes, head_dim)
        )
    context = jnp.concatenate(contexts, axis=0)
    partial_attn = jnp.dot(
        context,
        out_weight.reshape(heads_here * head_dim, features),
        preferred_element_type=jnp.float32,
    )
    partial_attn = partial_attn.reshape(group_size, req_count, span_rows, features)
    attn_rows = lax.psum_scatter(
        partial_attn.astype(jnp.bfloat16), "head", scatter_dimension=2, tiled=True
    ).astype(jnp.float32)
    residual_rows = dealt_rows.astype(jnp.float32) + attn_rows
    normed_rows = layer_norm(residual_rows, mlp_gain).astype(jnp.bfloat16)
    normed_all = lax.all_gather(normed_rows, "head", axis=2, tiled=True)
    inner = jax.nn.gelu(
        jnp.dot(
            normed_all.reshape(group_size * stretch_max, features),
            up_weight,
            preferred_element_type=jnp.float32,
        ),
        approximate=False,
    ).astype(jnp.bfloat16)
    partial_mlp = jnp.dot(inner, down_weight, preferred_element_type=jnp.float32).reshape(
        group_size, req_count, span_rows, features
    )
    mlp_rows = lax.psum_scatter(
        partial_mlp.astype(jnp.bfloat16), "head", scatter_dimension=2, tiled=True
    ).astype(jnp.float32)
    row_number = (
        jnp.arange(req_count, dtype=jnp.int32)[:, None] * head_count + head_index
    ) * stretch_rows + jnp.arange(stretch_rows, dtype=jnp.int32)[None, :]
    usable = row_number[None] < member_stretch[:, None, None]
    result = jnp.where(
        usable[..., None], residual_rows + mlp_rows, jnp.zeros((), jnp.float32)
    ).astype(jnp.bfloat16)
    returned = lax.all_to_all(result, "req", split_axis=1, concat_axis=0, tiled=True).reshape(
        requests, stretch_rows, features
    )
    inverse = jnp.argsort(req_order)
    layer_out = jnp.take(returned, inverse, axis=0)
    return (layer_out, relaid)


def solution(mesh):
    return jax.shard_map(
        local,
        mesh=mesh,
        in_specs=(
            P(None, ("req", "head"), None),
            P("req", None, "head", None, None),
            P(),
            P(),
            P(),
            P(),
            P(None, "head", None),
            P("head"),
            P("head", None, None),
            P(),
            P(None, "head"),
            P("head", None),
        ),
        out_specs=(P(None, ("req", "head"), None), P(None, "req", None, "head", None)),
        check_vma=False,
    )
```

profile of v0, /device:TPU:0, one launch (start us, length us, event | category | flops | bytes accessed | tf_op | source)
XLA Modules:
  0.0 427.9 jit_solution(1506799252785771041)
XLA Ops:
  7.2 0.8 compare_select_fusion.1
  8.0 1.4 gather_fusion
  10.1 1.5 gather_fusion.2
  12.4 4.2 all-to-all-start
  16.6 5.2 %slice_bitcast_fusion = (bf16[8,32,32,128]{3,2,1,0:T(8,128)(2,1)}, bf16[8,32,32,128]{3,2,1,0:T(8,128)(2,1)}) fusion(bf16[2,8,32,32,128]{4,3,2,1,0:T(8,128)(2,1)} %param.19), kind=kLoop, calls=%fused_computation.31 | loop fusion | bytes 8388608 | tf_op jit(solution)/shard_map/jit(_take)/Arg_0.9 | solution.py:84
  21.8 3.7 gather_fusion.6
  25.5 3.7 gather_fusion.3
  29.3 3.5 fusion.12
  32.8 2.1 copy.51
  35.6 6.5 %all-to-all-start.1 = ((bf16[1,8,32,32,128]{4,2,1,0,3:T(8,128)(2,1)}), bf16[1,8,32,32,128]{4,2,1,0,3:T(8,128)(2,1)}, u32[]{:S(2)}, u32[]{:S(2)}) async-start(bf16[1,8,32,32,128]{4,2,1,0,3:T(8,128)(2,1)} %copy.51), calls=%async_computation.1 | async-start | bytes 4194304 | tf_op jit(solution)/shard_map/all_to_all | solution.py:89
  45.6 1.3 iota_compare_fusion.1
  49.6 0.9 subtract_convert_fusion.1
  50.5 0.9 subtract_convert_fusion
  51.4 57.4 %all-to-all-done.1 = bf16[1,8,32,32,128]{4,2,1,0,3:T(8,128)(2,1)} async-done(((bf16[1,8,32,32,128]{4,2,1,0,3:T(8,128)(2,1)}), bf16[1,8,32,32,128]{4,2,1,0,3:T(8,128)(2,1)}, u32[]{:S(2)}, u32[]{:S(2)}) %all-to-all-start.1) | async-done | bytes 2097184 | tf_op jit(solution)/shard_map/all_to_all | solution.py:89
  108.8 2.0 copy.52
  110.9 1.9 copy.53
  112.8 4.5 %all-to-all-start.2 = ((bf16[1,8,256,4,128]{4,2,3,0,1:T(8,128)(2,1)}), bf16[1,8,256,4,128]{4,2,3,0,1:T(8,128)(2,1)}, u32[]{:S(2)}, u32[]{:S(2)}) async-start(bf16[1,8,256,4,128]{4,2,3,0,1:T(8,128)(2,1)} %bitcast.121), calls=%async_computation.2 | async-start | bytes 4194304 | tf_op jit(solution)/shard_map/all_to_all | solution.py:88
  117.5 2.1 convert_reduce_fusion
  121.3 1.8 fusion.21
  123.1 0.9 copy-done.12
  124.1 18.9 %all-to-all-done.2 = bf16[1,8,256,4,128]{4,2,3,0,1:T(8,128)(2,1)} async-done(((bf16[1,8,256,4,128]{4,2,3,0,1:T(8,128)(2,1)}), bf16[1,8,256,4,128]{4,2,3,0,1:T(8,128)(2,1)}, u32[]{:S(2)}, u32[]{:S(2)}) %all-to-all-start.2) | async-done | bytes 2097184 | tf_op jit(solution)/shard_map/all_to_all | solution.py:88
  143.0 2.9 copy.55
  146.6 2.2 fusion.122
  148.8 2.3 convolution_convert_fusion.3
  151.1 2.0 fusion.121
  153.1 2.4 convolution_convert_fusion.2
  156.4 2.9 copy.82
  159.3 4.5 %reshape.468 = bf16[64,16384]{1,0:T(8,128)(2,1)} reshape(bf16[64,2,4,2048]{3,2,1,0:T(4,128)(2,1)} %bitcast.123) | data formatting | bytes 4194304
  164.5 66.1 %reduce-scatter.7.cloned.1.call-done = bf16[8,16384]{1,0:T(8,128)(2,1)} async-done(((bf16[64,16384]{1,0:T(8,128)(2,1)}), bf16[8,16384]{1,0:T(8,128)(2,1)}) %reduce-scatter.7.cloned.1.call-update) | async-done | bytes 262160
  230.6 1.1 reshape.469
  232.4 0.9 multiply_convert_fusion
  233.3 2.1 copy.61
  235.5 3.6 all-to-all-start.4
  239.3 73.6 %all-gather.5.cloned.1.call-done = bf16[2,4,64,2048]{3,2,0,1:T(8,128)(2,1)} async-done(((bf16[2,4,8,2048]{3,2,0,1:T(8,128)(2,1)}), bf16[2,4,64,2048]{3,2,0,1:T(8,128)(2,1)}) %all-gather.5.cloned.1.call-update) | async-done | bytes 2097168 | tf_op jit(solution)/shard_map/all_gather | solution.py:132
  313.0 3.2 copy.59
  316.1 14.3 %convolution_convert_fusion = bf16[512,2048]{1,0:T(8,128)(2,1)} fusion(bf16[1024,2048]{1,0:T(8,128)(2,1)} %param.29, bf16[512,2048]{1,0:T(8,128)(2,1)} %bitcast.134, bf16[2048,1024]{1,0:T(8,128)(2,1)} %param.28), kind=kOutput, calls=%fused_computation.20 | convolution fusion | flops 4330094592 | bytes 12582912 | tf_op jit(solution)/shard_map/dot_general | solution.py:141
  330.4 4.5 %copy.81 = bf16[2,4,64,2048]{3,1,0,2:T(4,128)(2,1)} copy(bf16[2,4,64,2048]{3,2,1,0:T(8,128)(2,1)} %bitcast.135) | data formatting | bytes 4194304
  334.9 4.5 %reshape.470 = bf16[64,16384]{1,0:T(8,128)(2,1)} reshape(bf16[64,2,4,2048]{3,2,1,0:T(4,128)(2,1)} %bitcast.124) | data formatting | bytes 4194304
  339.4 1.0 sort.17
  340.8 1.9 copy.63
  342.7 3.6 all-to-all-start.5
  346.5 58.5 %reduce-scatter.9.cloned.1.call-done = bf16[8,16384]{1,0:T(8,128)(2,1)} async-done(((bf16[64,16384]{1,0:T(8,128)(2,1)}), bf16[8,16384]{1,0:T(8,128)(2,1)}) %reduce-scatter.9.cloned.1.call-update) | async-done | bytes 262160
  405.1 1.1 reshape.471
  406.2 1.0 select_convert_fusion
  407.2 3.7 all-to-all-start.3
  410.9 2.0 pad_maximum_fusion
  412.9 5.5 %copy.65 = bf16[4,2,2,256,4,128]{5,4,3,2,1,0:T(4,128)(2,1)} copy(bf16[4,2,2,256,4,128]{5,3,4,2,0,1:T(8,128)(2,1)S(1)} %pad_maximum_fusion) | data formatting | bytes 8388608 | tf_op jit(solution)/shard_map/stack | solution.py:97
  419.1 1.5 gather_fusion.5
  (93 shorter events, 15.7 us)
Async XLA Ops:
  7.2 114.1 %copy-start = (bf16[2048,4,192]{0,2,1:T(8,128)(2,1)S(1)}, bf16[2048,4,192]{0,2,1:T(8,128)(2,1)}, u32[]{:S(2)}) copy-start(bf16[2048,4,192]{0,2,1:T(8,128)(2,1)} %param.24) | copy-start | bytes 9437188
  12.4 22.5 %all-to-all-start = ((bf16[8,8,2048]{2,1,0:T(8,128)(2,1)}), bf16[8,8,2048]{2,1,0:T(8,128)(2,1)S(1)}, u32[]{:S(2)}, u32[]{:S(2)}) async-start(bf16[8,8,2048]{2,1,0:T(8,128)(2,1)} %broadcast_select_fusion.1), calls=%async_computation | async-start | bytes 524288 | tf_op jit(solution)/shard_map/all_to_all | solution.py:99
  34.9 8.0 %copy-start.17 = (s32[8]{0:T(128)S(1)}, s32[8]{0:T(128)}, u32[]{:S(2)}) copy-start(s32[8]{0:T(128)} %param.22) | copy-start | bytes 100
  34.9 8.1 %copy-start.2 = (s32[8]{0:T(128)S(1)}, s32[8]{0:T(128)}, u32[]{:S(2)}) copy-start(s32[8]{0:T(128)} %param.21) | copy-start | bytes 100
  34.9 8.7 %copy-start.3 = (s32[8]{0:T(128)S(1)}, s32[8]{0:T(128)}, u32[]{:S(2)}) copy-start(s32[8]{0:T(128)} %param.20) | copy-start | bytes 100
  34.9 9.3 %copy-start.15 = (bf16[2048]{0:T(1024)(128)(2,1)S(1)}, bf16[2048]{0:T(1024)(128)(2,1)}, u32[]{:S(2)}) copy-start(bf16[2048]{0:T(1024)(128)(2,1)} %param.23) | copy-start | bytes 12292
  34.9 0.7 copy-start.5
  35.6 73.2 %all-to-all-start.1 = ((bf16[1,8,32,32,128]{4,2,1,0,3:T(8,128)(2,1)}), bf16[1,8,32,32,128]{4,2,1,0,3:T(8,128)(2,1)}, u32[]{:S(2)}, u32[]{:S(2)}) async-start(bf16[1,8,32,32,128]{4,2,1,0,3:T(8,128)(2,1)} %copy.51), calls=%async_computation.1 | async-start | bytes 4194304 | tf_op jit(solution)/shard_map/all_to_all | solution.py:89
  42.1 75.4 %all-gather.3.cloned.1.call-start = ((), (), s32[]{:S(2)}) async-start(), calls=%async_computation.8 | async-start | bytes 2359296 | tf_op jit(solution)/shard_map/all_gather | solution.py:102
  112.8 30.2 %all-to-all-start.2 = ((bf16[1,8,256,4,128]{4,2,3,0,1:T(8,128)(2,1)}), bf16[1,8,256,4,128]{4,2,3,0,1:T(8,128)(2,1)}, u32[]{:S(2)}, u32[]{:S(2)}) async-start(bf16[1,8,256,4,128]{4,2,3,0,1:T(8,128)(2,1)} %bitcast.121), calls=%async_computation.2 | async-start | bytes 4194304 | tf_op jit(solution)/shard_map/all_to_all | solution.py:88
  117.2 113.3 %reduce-scatter.7.cloned.1.call-start = ((), (), s32[]{:S(2)}) async-start(), calls=%async_computation.10 | async-start | bytes 2359296
  117.5 2.2 copy-start.4
  123.1 0.9 copy-start.12
  124.0 22.6 %copy-start.11 = (f32[256,512]{1,0:T(8,128)S(1)}, f32[256,512]{1,0:T(8,128)}, u32[]{:S(2)}) copy-start(f32[256,512]{1,0:T(8,128)} %subtract_convert_fusion.1) | copy-start | bytes 1572868
  124.1 22.6 %copy-start.18 = (f32[4]{0:T(128)S(1)}, f32[4]{0:T(128)}, u32[]{:S(2)}) copy-start(f32[4]{0:T(128)} %param.25) | copy-start | bytes 52
  146.6 4.5 %copy-start.13 = (bf16[256,4,128]{0,2,1:T(8,128)(2,1)}, bf16[256,4,128]{0,2,1:T(8,128)(2,1)S(1)}, u32[]{:S(2)}) copy-start(bf16[256,4,128]{0,2,1:T(8,128)(2,1)S(1)} %get-tuple-element.12) | copy-start | bytes 786436
  146.6 2.2 copy-start.14
  148.8 2.3 copy-start.10
  153.1 2.5 copy-start.9
  163.8 0.7 copy-start.16
  163.8 68.0 %copy-start.6 = (bf16[8,8,2048]{2,1,0:T(8,128)(2,1)S(1)}, bf16[8,8,2048]{2,1,0:T(8,128)(2,1)}, u32[]{:S(2)}) copy-start(bf16[8,8,2048]{2,1,0:T(8,128)(2,1)} %copy-done.5) | copy-start | bytes 786436
  163.8 69.5 %copy-start.7 = (bf16[1,8,32,32,128]{4,3,2,1,0:T(8,128)(2,1)S(1)}, bf16[1,8,32,32,128]{4,3,2,1,0:T(8,128)(2,1)}, u32[]{:S(2)}) copy-start(bf16[1,8,32,32,128]{4,3,2,1,0:T(8,128)(2,1)} %get-tuple-element.17) | copy-start | bytes 6291460
  163.8 149.2 %all-gather.5.cloned.1.call-start = ((), (), s32[]{:S(2)}) async-start(), calls=%async_computation.9 | async-start | bytes 2359296 | tf_op jit(solution)/shard_map/all_gather | solution.py:132
  235.5 104.9 %all-to-all-start.4 = ((bf16[1,8,32,32,128]{4,2,1,0,3:T(8,128)(2,1)}), bf16[1,8,32,32,128]{4,2,1,0,3:T(8,128)(2,1)S(1)}, u32[]{:S(2)}, u32[]{:S(2)}) async-start(bf16[1,8,32,32,128]{4,2,1,0,3:T(8,128)(2,1)} %copy.61), calls=%async_computation.4 | async-start | bytes 4194304 | tf_op jit(solution)/shard_map/all_to_all | solution.py:89
  239.1 166.0 %reduce-scatter.9.cloned.1.call-start = ((), (), s32[]{:S(2)}) async-start(), calls=%async_computation.11 | async-start | bytes 2359296
  342.7 64.5 %all-to-all-start.5 = ((bf16[1,8,256,4,128]{4,2,3,0,1:T(8,128)(2,1)}), bf16[1,8,256,4,128]{4,2,3,0,1:T(8,128)(2,1)S(1)}, u32[]{:S(2)}, u32[]{:S(2)}) async-start(bf16[1,8,256,4,128]{4,2,3,0,1:T(8,128)(2,1)} %bitcast.44), calls=%async_computation.5 | async-start | bytes 4194304 | tf_op jit(solution)/shard_map/all_to_all | solution.py:88
  407.2 11.2 %all-to-all-start.3 = ((bf16[2,4,8,2048]{3,2,0,1:T(8,128)(2,1)}), bf16[2,4,8,2048]{3,2,0,1:T(8,128)(2,1)S(1)}, u32[]{:S(2)}, u32[]{:S(2)}) async-start(bf16[2,4,8,2048]{3,2,0,1:T(8,128)(2,1)} %select_convert_fusion), calls=%async_computation.3 | async-start | bytes 524288 | tf_op jit(solution)/shard_map/all_to_all | solution.py:154
  412.9 8.5 %copy-start.1 = (bf16[2048,4,192]{0,2,1:T(8,128)(2,1)S(1)}, bf16[2048,4,192]{0,2,1:T(8,128)(2,1)}, u32[]{:S(2)}) copy-start(bf16[2048,4,192]{0,2,1:T(8,128)(2,1)} %param.24) | copy-start | bytes 9437188
  418.4 0.7 copy-start.8
Sparse Core Ops, SparseCore 0:
  45.7 71.0 all-gather.2
  163.9 66.6 reduce-scatter.6
  233.4 79.4 all-gather.4
  339.5 65.4 reduce-scatter.8
where the time goes:
time: 429 us; the launch traced here: 428 us
  waiting for transfers between devices  275 us (64%)
  local copies, waits for them, and re-layouts  63.7 us (15%)
  starting transfers between devices  26.6 us (6%)
  matrix products  25.6 us (6%)
  other arithmetic  22.4 us (5%)
  between operations  14.2 us (3%)
    unnamed x6, waiting for transfers between devices  125 us
    all_gather x1, waiting for transfers between devices, local(): normed_all = lax.all_gather(normed_rows, 'head', axis=2, tiled=True)  73.6 us
    all_to_all x2, waiting for transfers between devices, local(): lax.all_to_all(dealt_cache, 'head', split_axis=3, concat_axis=2, tiled=True)  57.4 us
    unnamed x44, local copies, waits for them, and re-layouts  21.7 us
    all_to_all x2, waiting for transfers between devices, local(): lax.all_to_all(lax.all_to_all(dealt_cache, 'head', split_axis=3, concat_a...  18.9 us
    dot_general x1, matrix products, local(): jnp.dot(inner, down_weight, preferred_element_type=jnp.float32)  14.3 us
    all_to_all x2, starting transfers between devices, local(): lax.all_to_all(dealt_cache, 'head', split_axis=3, concat_axis=2, tiled=True)  10.1 us
  transfers between devices with their start and end apart: 10, of which 5 were waited for; matrix products, arithmetic and copies ran while one was open for 18% of the time, Pallas kernels for 0%

commit v1 on v0

--- a/solution.py
+++ b/solution.py
@@ -3,6 +3,7 @@
 import jax.numpy as jnp
 from jax import lax
 from jax.sharding import PartitionSpec as P
+from jax.lax import axis_index, axis_size, ppermute
 
 EPSILON = 1e-05
 
@@ -129,7 +130,31 @@
     ).astype(jnp.float32)
     residual_rows = dealt_rows.astype(jnp.float32) + attn_rows
     normed_rows = layer_norm(residual_rows, mlp_gain).astype(jnp.bfloat16)
-    normed_all = lax.all_gather(normed_rows, "head", axis=2, tiled=True)
+
+    def orders_keep_up(target, dimension_no=2):
+        named_axis = "head"
+        finding, r_now, built = (
+            axis_size(named_axis),
+            axis_index(named_axis),
+            target.shape[dimension_no],
+        )
+        passed, all_values = (target, 1)
+        while all_values < finding:
+            passed = jnp.concatenate(
+                [
+                    passed,
+                    ppermute(
+                        passed,
+                        named_axis,
+                        [(ix, (ix - all_values) % finding) for ix in range(finding)],
+                    ),
+                ],
+                axis=dimension_no,
+            )
+            all_values = 2 * all_values
+        return jnp.roll(passed, shift=r_now * built, axis=dimension_no)
+
+    normed_all = orders_keep_up(normed_rows)
     inner = jax.nn.gelu(
         jnp.dot(
             normed_all.reshape(group_size * stretch_max, features),

time: 429 us -> 448 us (1.044)
  starting transfers between devices: 26.6 us -> 35.5 us
  local copies, waits for them, and re-layouts: 63.7 us -> 72.3 us
    all_gather x1 -> x0, waiting for transfers between devices: 73.6 us -> none  [local(): normed_all = lax.all_gather(normed_rows, 'head', axis=2, tiled=True)]
    ppermute x0 -> x3, waiting for transfers between devices: none -> 71.2 us  [orders_keep_up(): ppermute(passed, named_axis, [(ix, (ix - all_values) % finding) for ix in...]
    unnamed x44 -> x54, local copies, waits for them, and re-layouts: 21.7 us -> 27.9 us
    ppermute x0 -> x3, starting transfers between devices: none -> 4.98 us  [orders_keep_up(): ppermute(passed, named_axis, [(ix, (ix - all_values) % finding) for ix in...]
    unnamed x6 -> x5, waiting for transfers between devices: 125 us -> 128 us
  transfers between devices with their start and end apart: 10 -> 12, of which waited for: 5 -> 7; matrix products, arithmetic and copies ran while one was open for 18% -> 19% of each run, Pallas kernels for 0% -> 0%
where the time goes in v1:
time: 448 us; the launch traced here: 447 us
  waiting for transfers between devices  276 us (62%)
  local copies, waits for them, and re-layouts  72.3 us (16%)
  starting transfers between devices  35.5 us (8%)
  matrix products  25.6 us (6%)
  other arithmetic  23.6 us (5%)
  between operations  14.2 us (3%)
    unnamed x5, waiting for transfers between devices  128 us
    ppermute x3, waiting for transfers between devices, orders_keep_up(): ppermute(passed, named_axis, [(ix, (ix - all_values) % finding) for ix in...  71.2 us
    all_to_all x2, waiting for transfers between devices, local(): lax.all_to_all(dealt_cache, 'head', split_axis=3, concat_axis=2, tiled=True)  57.4 us
    unnamed x54, local copies, waits for them, and re-layouts  27.9 us
    all_to_all x2, waiting for transfers between devices, local(): lax.all_to_all(lax.all_to_all(dealt_cache, 'head', split_axis=3, concat_a...  18.9 us
    all_to_all x2, starting transfers between devices, local(): lax.all_to_all(dealt_cache, 'head', split_axis=3, concat_axis=2, tiled=True)  14.3 us
    dot_general x1, matrix products, local(): jnp.dot(inner, down_weight, preferred_element_type=jnp.float32)  14.3 us
  transfers between devices with their start and end apart: 12, of which 7 were waited for; matrix products, arithmetic and copies ran while one was open for 19% of the time, Pallas kernels for 0%

profile of v1, /device:TPU:0, one launch (start us, length us, event | category | flops | bytes accessed | tf_op | source)
XLA Modules:
  0.0 446.8 jit_solution(551083122537176693)
XLA Ops:
  8.0 1.4 gather_fusion
  10.1 1.5 gather_fusion.2
  12.4 4.2 all-to-all-start
  16.6 5.2 %slice_bitcast_fusion = (bf16[8,32,32,128]{3,2,1,0:T(8,128)(2,1)}, bf16[8,32,32,128]{3,2,1,0:T(8,128)(2,1)}) fusion(bf16[2,8,32,32,128]{4,3,2,1,0:T(8,128)(2,1)} %param.19), kind=kLoop, calls=%fused_computation.31 | loop fusion | bytes 8388608 | tf_op jit(solution)/shard_map/jit(_take)/Arg_0.9 | solution.py:85
  21.8 3.7 gather_fusion.6
  25.5 3.7 gather_fusion.3
  29.3 3.5 fusion.12
  32.8 2.1 copy.51
  35.7 6.5 %all-to-all-start.1 = ((bf16[1,8,32,32,128]{4,2,1,0,3:T(8,128)(2,1)}), bf16[1,8,32,32,128]{4,2,1,0,3:T(8,128)(2,1)}, u32[]{:S(2)}, u32[]{:S(2)}) async-start(bf16[1,8,32,32,128]{4,2,1,0,3:T(8,128)(2,1)} %copy.51), calls=%async_computation.1 | async-start | bytes 4194304 | tf_op jit(solution)/shard_map/all_to_all | solution.py:90
  45.7 1.3 iota_compare_fusion.1
  51.5 57.4 %all-to-all-done.1 = bf16[1,8,32,32,128]{4,2,1,0,3:T(8,128)(2,1)} async-done(((bf16[1,8,32,32,128]{4,2,1,0,3:T(8,128)(2,1)}), bf16[1,8,32,32,128]{4,2,1,0,3:T(8,128)(2,1)}, u32[]{:S(2)}, u32[]{:S(2)}) %all-to-all-start.1) | async-done | bytes 2097184 | tf_op jit(solution)/shard_map/all_to_all | solution.py:90
  108.9 2.0 copy.52
  110.9 1.9 copy.53
  112.8 4.4 all-to-all-start.2
  117.5 2.1 convert_reduce_fusion
  121.3 1.8 fusion.21
  124.1 18.9 %all-to-all-done.2 = bf16[1,8,256,4,128]{4,2,3,0,1:T(8,128)(2,1)} async-done(((bf16[1,8,256,4,128]{4,2,3,0,1:T(8,128)(2,1)}), bf16[1,8,256,4,128]{4,2,3,0,1:T(8,128)(2,1)}, u32[]{:S(2)}, u32[]{:S(2)}) %all-to-all-start.2) | async-done | bytes 2097184 | tf_op jit(solution)/shard_map/all_to_all | solution.py:89
  143.0 2.9 copy.55
  146.6 2.2 fusion.122
  148.8 2.3 convolution_convert_fusion.3
  151.1 2.0 fusion.121
  153.1 2.4 convolution_convert_fusion.2
  156.4 2.9 copy.83
  159.3 4.4 reshape.468
  164.4 65.8 %reduce-scatter.7.cloned.1.call-done = bf16[8,16384]{1,0:T(8,128)(2,1)} async-done(((bf16[64,16384]{1,0:T(8,128)(2,1)}), bf16[8,16384]{1,0:T(8,128)(2,1)}) %reduce-scatter.7.cloned.1.call-update) | async-done | bytes 262160
  230.3 1.1 reshape.469
  233.0 2.0 collective-permute-start
  235.0 5.1 %collective-permute-done = bf16[2,4,8,2048]{3,2,0,1:T(8,128)(2,1)S(1)} collective-permute-done((bf16[2,4,8,2048]{3,2,0,1:T(8,128)(2,1)S(1)}, bf16[2,4,8,2048]{3,2,0,1:T(8,128)(2,1)S(1)}, u32[]{:S(2)}, u32[]{:S(2)}) %collective-permute-start) | collective-permute-done | bytes 262176 | tf_op jit(solution)/shard_map/ppermute | solution.py:146
  240.2 1.7 collective-permute-start.1
  241.9 9.8 %collective-permute-done.1 = bf16[2,4,16,2048]{3,2,0,1:T(8,128)(2,1)S(1)} collective-permute-done((bf16[2,4,16,2048]{3,2,0,1:T(8,128)(2,1)S(1)}, bf16[2,4,16,2048]{3,2,0,1:T(8,128)(2,1)S(1)}, u32[]{:S(2)}, u32[]{:S(2)}) %collective-permute-start.1) | collective-permute-done | bytes 524320 | tf_op jit(solution)/shard_map/ppermute | solution.py:146
  252.8 1.2 collective-permute-start.2
  254.1 2.1 copy.61
  256.2 7.8 %all-to-all-start.4 = ((bf16[1,8,32,32,128]{4,2,1,0,3:T(8,128)(2,1)}), bf16[1,8,32,32,128]{4,2,1,0,3:T(8,128)(2,1)S(1)}, u32[]{:S(2)}, u32[]{:S(2)}) async-start(bf16[1,8,32,32,128]{4,2,1,0,3:T(8,128)(2,1)} %copy.61), calls=%async_computation.4 | async-start | bytes 4194304 | tf_op jit(solution)/shard_map/all_to_all | solution.py:90
  265.6 56.2 %collective-permute-done.2 = bf16[2,4,32,2048]{3,2,0,1:T(8,128)(2,1)} collective-permute-done((bf16[2,4,32,2048]{3,2,0,1:T(8,128)(2,1)}, bf16[2,4,32,2048]{3,2,0,1:T(8,128)(2,1)}, u32[]{:S(2)}, u32[]{:S(2)}) %collective-permute-start.2) | collective-permute-done | bytes 1048608 | tf_op jit(solution)/shard_map/ppermute | solution.py:146
  321.8 2.3 constant_dynamic-update-slice_fusion.4
  326.4 2.3 constant_dynamic-update-slice_fusion
  328.7 1.7 constant_dynamic-slice_fusion
  330.5 1.5 copy.59
  331.9 14.3 %convolution_convert_fusion = bf16[512,2048]{1,0:T(8,128)(2,1)} fusion(bf16[1024,2048]{1,0:T(8,128)(2,1)} %param.29, bf16[512,2048]{1,0:T(8,128)(2,1)} %bitcast.135, bf16[2048,1024]{1,0:T(8,128)(2,1)} %param.28), kind=kOutput, calls=%fused_computation.20 | convolution fusion | flops 4330094592 | bytes 12582912 | tf_op jit(solution)/shard_map/dot_general | solution.py:166
  346.2 4.5 %copy.82 = bf16[2,4,64,2048]{3,1,0,2:T(4,128)(2,1)} copy(bf16[2,4,64,2048]{3,2,1,0:T(8,128)(2,1)} %bitcast.136) | data formatting | bytes 4194304
  350.7 4.4 reshape.470
  356.6 1.9 copy.63
  358.5 3.9 all-to-all-start.5
  362.6 61.6 %reduce-scatter.9.cloned.1.call-done = bf16[8,16384]{1,0:T(8,128)(2,1)} async-done(((bf16[64,16384]{1,0:T(8,128)(2,1)}), bf16[8,16384]{1,0:T(8,128)(2,1)}) %reduce-scatter.9.cloned.1.call-update) | async-done | bytes 262160
  426.4 3.4 all-to-all-start.3
  429.8 2.0 pad_maximum_fusion
  431.8 5.5 %copy.65 = bf16[4,2,2,256,4,128]{5,4,3,2,1,0:T(4,128)(2,1)} copy(bf16[4,2,2,256,4,128]{5,3,4,2,0,1:T(8,128)(2,1)S(1)} %pad_maximum_fusion) | data formatting | bytes 8388608 | tf_op jit(solution)/shard_map/stack | solution.py:98
  438.0 1.5 gather_fusion.5
  (110 shorter events, 28.0 us)
Async XLA Ops:
  7.2 114.1 %copy-start = (bf16[2048,4,192]{0,2,1:T(8,128)(2,1)S(1)}, bf16[2048,4,192]{0,2,1:T(8,128)(2,1)}, u32[]{:S(2)}) copy-start(bf16[2048,4,192]{0,2,1:T(8,128)(2,1)} %param.24) | copy-start | bytes 9437188
  12.4 22.5 %all-to-all-start = ((bf16[8,8,2048]{2,1,0:T(8,128)(2,1)}), bf16[8,8,2048]{2,1,0:T(8,128)(2,1)S(1)}, u32[]{:S(2)}, u32[]{:S(2)}) async-start(bf16[8,8,2048]{2,1,0:T(8,128)(2,1)} %broadcast_select_fusion.1), calls=%async_computation | async-start | bytes 524288 | tf_op jit(solution)/shard_map/all_to_all | solution.py:100
  34.9 8.0 %copy-start.19 = (s32[8]{0:T(128)S(1)}, s32[8]{0:T(128)}, u32[]{:S(2)}) copy-start(s32[8]{0:T(128)} %param.22) | copy-start | bytes 100
  34.9 8.1 %copy-start.2 = (s32[8]{0:T(128)S(1)}, s32[8]{0:T(128)}, u32[]{:S(2)}) copy-start(s32[8]{0:T(128)} %param.21) | copy-start | bytes 100
  34.9 8.7 %copy-start.3 = (s32[8]{0:T(128)S(1)}, s32[8]{0:T(128)}, u32[]{:S(2)}) copy-start(s32[8]{0:T(128)} %param.20) | copy-start | bytes 100
  34.9 9.3 %copy-start.17 = (bf16[2048]{0:T(1024)(128)(2,1)S(1)}, bf16[2048]{0:T(1024)(128)(2,1)}, u32[]{:S(2)}) copy-start(bf16[2048]{0:T(1024)(128)(2,1)} %param.23) | copy-start | bytes 12292
  35.0 0.7 copy-start.5
  35.7 73.2 %all-to-all-start.1 = ((bf16[1,8,32,32,128]{4,2,1,0,3:T(8,128)(2,1)}), bf16[1,8,32,32,128]{4,2,1,0,3:T(8,128)(2,1)}, u32[]{:S(2)}, u32[]{:S(2)}) async-start(bf16[1,8,32,32,128]{4,2,1,0,3:T(8,128)(2,1)} %copy.51), calls=%async_computation.1 | async-start | bytes 4194304 | tf_op jit(solution)/shard_map/all_to_all | solution.py:90
  42.2 75.3 %all-gather.2.cloned.1.call-start = ((), (), s32[]{:S(2)}) async-start(), calls=%async_computation.8 | async-start | bytes 2359296 | tf_op jit(solution)/shard_map/all_gather | solution.py:103
  112.8 30.2 %all-to-all-start.2 = ((bf16[1,8,256,4,128]{4,2,3,0,1:T(8,128)(2,1)}), bf16[1,8,256,4,128]{4,2,3,0,1:T(8,128)(2,1)}, u32[]{:S(2)}, u32[]{:S(2)}) async-start(bf16[1,8,256,4,128]{4,2,3,0,1:T(8,128)(2,1)} %bitcast.122), calls=%async_computation.2 | async-start | bytes 4194304 | tf_op jit(solution)/shard_map/all_to_all | solution.py:89
  117.3 113.0 %reduce-scatter.7.cloned.1.call-start = ((), (), s32[]{:S(2)}) async-start(), calls=%async_computation.9 | async-start | bytes 2359296
  117.5 2.2 copy-start.4
  123.1 0.9 copy-start.14
  124.1 22.6 %copy-start.13 = (f32[256,512]{1,0:T(8,128)S(1)}, f32[256,512]{1,0:T(8,128)}, u32[]{:S(2)}) copy-start(f32[256,512]{1,0:T(8,128)} %subtract_convert_fusion.1) | copy-start | bytes 1572868
  124.1 22.6 %copy-start.20 = (f32[4]{0:T(128)S(1)}, f32[4]{0:T(128)}, u32[]{:S(2)}) copy-start(f32[4]{0:T(128)} %param.25) | copy-start | bytes 52
  146.6 4.5 %copy-start.15 = (bf16[256,4,128]{0,2,1:T(8,128)(2,1)}, bf16[256,4,128]{0,2,1:T(8,128)(2,1)S(1)}, u32[]{:S(2)}) copy-start(bf16[256,4,128]{0,2,1:T(8,128)(2,1)S(1)} %get-tuple-element.14) | copy-start | bytes 786436
  146.6 2.2 copy-start.16
  148.8 2.3 copy-start.12
  153.1 2.5 copy-start.11
  163.8 0.7 copy-start.18
  163.8 67.7 %copy-start.6 = (bf16[8,8,2048]{2,1,0:T(8,128)(2,1)S(1)}, bf16[8,8,2048]{2,1,0:T(8,128)(2,1)}, u32[]{:S(2)}) copy-start(bf16[8,8,2048]{2,1,0:T(8,128)(2,1)} %copy-done.5) | copy-start | bytes 786436
  232.1 22.0 %copy-start.7 = (bf16[1,8,32,32,128]{4,3,2,1,0:T(8,128)(2,1)S(1)}, bf16[1,8,32,32,128]{4,3,2,1,0:T(8,128)(2,1)}, u32[]{:S(2)}) copy-start(bf16[1,8,32,32,128]{4,3,2,1,0:T(8,128)(2,1)} %get-tuple-element.19) | copy-start | bytes 6291460
  233.0 18.7 %copy-start.8 = (bf16[2,4,8,2048]{3,2,0,1:T(8,128)(2,1)}, bf16[2,4,8,2048]{3,2,0,1:T(8,128)(2,1)S(1)}, u32[]{:S(2)}) copy-start(bf16[2,4,8,2048]{3,2,0,1:T(8,128)(2,1)S(1)} %get-tuple-element.8) | copy-start | bytes 786436
  233.0 7.1 %collective-permute-start = (bf16[2,4,8,2048]{3,2,0,1:T(8,128)(2,1)S(1)}, bf16[2,4,8,2048]{3,2,0,1:T(8,128)(2,1)S(1)}, u32[]{:S(2)}, u32[]{:S(2)}) collective-permute-start(bf16[2,4,8,2048]{3,2,0,1:T(8,128)(2,1)S(1)} %get-tuple-element.8), channel_id=1, source_target_pairs={{0,7},{1,0},{2,1},{3,2},{4,3},{5,4},{6,5},{7,6},{8,15},{9,8},{10,9... | collective-permute-start | bytes 786440 | tf_op jit(solution)/shard_map/ppermute | solution.py:146
  240.2 11.6 %collective-permute-start.1 = (bf16[2,4,16,2048]{3,2,0,1:T(8,128)(2,1)S(1)}, bf16[2,4,16,2048]{3,2,0,1:T(8,128)(2,1)S(1)}, u32[]{:S(2)}, u32[]{:S(2)}) collective-permute-start(bf16[2,4,16,2048]{3,2,0,1:T(8,128)(2,1)S(1)} %pad_maximum_fusion.2), channel_id=1, source_target_pairs={{0,6},{1,7},{2,0},{3,1},{4,2},{5,3},{6,4},{7,5},{8,14},{9,15},{10,... | collective-permute-start | bytes 1572872 | tf_op jit(solution)/shard_map/ppermute | solution.py:146
  252.8 69.0 %collective-permute-start.2 = (bf16[2,4,32,2048]{3,2,0,1:T(8,128)(2,1)}, bf16[2,4,32,2048]{3,2,0,1:T(8,128)(2,1)}, u32[]{:S(2)}, u32[]{:S(2)}) collective-permute-start(bf16[2,4,32,2048]{3,2,0,1:T(8,128)(2,1)} %pad_maximum_fusion.1), channel_id=1, source_target_pairs={{0,4},{1,5},{2,6},{3,7},{4,0},{5,1},{6,2},{7,3},{8,12},{9,13},{10,... | collective-permute-start | bytes 3145736 | tf_op jit(solution)/shard_map/ppermute | solution.py:146
  256.2 100.0 %all-to-all-start.4 = ((bf16[1,8,32,32,128]{4,2,1,0,3:T(8,128)(2,1)}), bf16[1,8,32,32,128]{4,2,1,0,3:T(8,128)(2,1)S(1)}, u32[]{:S(2)}, u32[]{:S(2)}) async-start(bf16[1,8,32,32,128]{4,2,1,0,3:T(8,128)(2,1)} %copy.61), calls=%async_computation.4 | async-start | bytes 4194304 | tf_op jit(solution)/shard_map/all_to_all | solution.py:90
  264.0 160.2 %reduce-scatter.9.cloned.1.call-start = ((), (), s32[]{:S(2)}) async-start(), calls=%async_computation.10 | async-start | bytes 2359296
  264.0 60.1 %copy-start.9 = (bf16[2,4,8,2048]{3,2,0,1:T(8,128)(2,1)S(1)}, bf16[2,4,8,2048]{3,2,0,1:T(8,128)(2,1)}, u32[]{:S(2)}) copy-start(bf16[2,4,8,2048]{3,2,0,1:T(8,128)(2,1)} %copy-done.8) | copy-start | bytes 786436
  358.5 67.8 %all-to-all-start.5 = ((bf16[1,8,256,4,128]{4,2,3,0,1:T(8,128)(2,1)}), bf16[1,8,256,4,128]{4,2,3,0,1:T(8,128)(2,1)S(1)}, u32[]{:S(2)}, u32[]{:S(2)}) async-start(bf16[1,8,256,4,128]{4,2,3,0,1:T(8,128)(2,1)} %bitcast.44), calls=%async_computation.5 | async-start | bytes 4194304 | tf_op jit(solution)/shard_map/all_to_all | solution.py:89
  426.4 10.9 %all-to-all-start.3 = ((bf16[2,4,8,2048]{3,2,0,1:T(8,128)(2,1)}), bf16[2,4,8,2048]{3,2,0,1:T(8,128)(2,1)S(1)}, u32[]{:S(2)}, u32[]{:S(2)}) async-start(bf16[2,4,8,2048]{3,2,0,1:T(8,128)(2,1)} %select_convert_fusion), calls=%async_computation.3 | async-start | bytes 524288 | tf_op jit(solution)/shard_map/all_to_all | solution.py:179
  431.7 8.5 %copy-start.1 = (bf16[2048,4,192]{0,2,1:T(8,128)(2,1)S(1)}, bf16[2048,4,192]{0,2,1:T(8,128)(2,1)}, u32[]{:S(2)}) copy-start(bf16[2048,4,192]{0,2,1:T(8,128)(2,1)} %param.24) | copy-start | bytes 9437188
  437.3 0.7 copy-start.10
Sparse Core Ops, SparseCore 0:
  45.8 71.0 all-gather.1
  163.9 66.3 reduce-scatter.6
  355.3 68.8 reduce-scatter.8
